TPU v7x, 32 devices: a whole 2x2x4 slice. The times are simulated.
32 devices in a mesh: rep: 2 (over y), tp: 8 (over z, x), sub: 2 (over core).
Axes of the slice: x: 2, y: 2, z: 4, core: 2. Of those that a mesh axis runs over, the one named last changes fastest.
Arguments:
- queries: bfloat16 [2, 16, 16384], P(None, ('rep', 'sub'), 'tp'), parts along dimension 1, may hold values from -53 to 53
- prefix_kv: bfloat16 [2, 16384, 1024], P(None, ('rep', 'tp')), parts along dimension 1, may hold values from -6 to 6
- tail_kv: bfloat16 [2, 16, 1024, 1024], P(None, ('rep', 'sub'), 'tp'), parts along dimension 1, may hold values from -6 to 6
- tail_lengths: int32 [16], P(('rep', 'sub')), parts along dimension 0, may hold values from 1 to 1024, as said below
- fresh_kv: bfloat16 [2, 2, 16, 1024], P(None, None, ('rep', 'sub')), parts along dimension 2, may hold values from -6 to 6
- out_weight: bfloat16 [16384, 16384], P('tp', 'sub'), may hold values from -0.5 to 0.5
- scale_in: int32 [128], replicated, may hold values from 9 to 14
- scale_out: int32 [128], replicated, may hold values from 5 to 10
- residual: bfloat16 [2, 16, 16384], P(None, 'rep', 'sub'), parts along dimension 1, may hold values from -1.5 to 1.5
Outputs:
- hidden: bfloat16 [2, 16, 16384], P(None, 'rep', 'sub'), parts along dimension 1
There are 2 independent parts, one for each index of `rep`. A program takes and returns all parts, laid end to end along the dimension named above; an argument that names none is the same for every part. Nothing has to cross between parts.
Inputs may be any that keep to these rules, and one draw needn't show every extreme that they name: `tail_lengths`: some sample's tail reaches 1024 tokens.
All inputs are finite; a program needn't handle non-finite values.
Results may differ from a plain program's by a relative error of at most 0.0065.
Values may be sent and summed in bfloat16 or wider, within the bound.
No kernel may reach another device: no remote copies, remote signals or barrier semaphores. Data moves between devices by JAX's collectives and lax.ppermute only.
A program may use at most 192 MiB of HBM per device.

v0:
```python
import math
import jax
import jax.numpy as jnp
from jax import lax
from jax.sharding import PartitionSpec as P

DH = 128
NEG_FILL = -1e30


def per_device(
    queries, prefix_kv, tail_kv, tail_lengths, fresh_kv, out_weight, scale_in, scale_out, residual
):
    steps_n, rows_dev, width_dev = queries.shape
    heads_dev = width_dev // DH
    tp_count = lax.axis_size("tp")
    tp_rank = lax.axis_index("tp")
    sub_rank = lax.axis_index("sub")
    kv_heads = prefix_kv.shape[2] // DH
    copies = tp_count // kv_heads
    kv_group = tp_rank // copies
    prefix_dev = prefix_kv.shape[1]
    tail_dev = tail_kv.shape[2]
    score_scale = 1.0 / math.sqrt(DH)
    own_query = queries.reshape(steps_n, rows_dev, heads_dev, DH)
    own_fresh = lax.dynamic_slice_in_dim(fresh_kv, kv_group * DH, DH, 3)
    fresh_live = jnp.arange(steps_n)[None, :] <= jnp.arange(steps_n)[:, None]
    own_fresh_scores = (
        jnp.einsum("sbhd,ubd->sbhu", own_query, own_fresh[0], preferred_element_type=jnp.float32)
        * score_scale
    )
    own_fresh_scores = jnp.where(fresh_live[:, None, None, :], own_fresh_scores, NEG_FILL)
    spread_prompt = jnp.repeat(
        prefix_kv.reshape(2, prefix_dev, kv_heads, DH), copies, axis=2
    ).reshape(2, prefix_dev, tp_count * DH)
    spread_tail = jnp.repeat(
        tail_kv.reshape(2 * rows_dev, tail_dev, kv_heads, DH), copies, axis=2
    ).reshape(2 * rows_dev, tail_dev, tp_count * DH)
    moved_prompt, moved_tail = (
        lax.all_to_all(spread_prompt, "tp", split_axis=2, concat_axis=1, tiled=True),
        lax.all_to_all(spread_tail, "tp", split_axis=2, concat_axis=1, tiled=True),
    )
    tail_full = moved_tail.reshape(2, rows_dev, tail_dev * tp_count, DH)
    prompt_scores = (
        jnp.einsum("sbhd,pd->sbhp", own_query, moved_prompt[0], preferred_element_type=jnp.float32)
        * score_scale
    )
    tail_scores = (
        jnp.einsum("sbhd,btd->sbht", own_query, tail_full[0], preferred_element_type=jnp.float32)
        * score_scale
    )
    tail_live = jnp.arange(tail_dev * tp_count)[None, :] < tail_lengths[:, None]
    tail_scores = jnp.where(tail_live[None, :, None, :], tail_scores, NEG_FILL)
    peak = jnp.maximum(
        jnp.maximum(prompt_scores.max(-1), tail_scores.max(-1)), own_fresh_scores.max(-1)
    )
    prompt_weights = jnp.exp(prompt_scores - peak[..., None])
    tail_weights = jnp.exp(tail_scores - peak[..., None])
    fresh_weights = jnp.exp(own_fresh_scores - peak[..., None])
    mass = prompt_weights.sum(-1) + tail_weights.sum(-1) + fresh_weights.sum(-1)
    numer = jnp.einsum(
        "sbhp,pd->sbhd",
        prompt_weights.astype(jnp.bfloat16),
        moved_prompt[1],
        preferred_element_type=jnp.float32,
    )
    numer = numer + jnp.einsum(
        "sbht,btd->sbhd",
        tail_weights.astype(jnp.bfloat16),
        tail_full[1],
        preferred_element_type=jnp.float32,
    )
    numer = numer + jnp.einsum(
        "sbhu,ubd->sbhd",
        fresh_weights.astype(jnp.bfloat16),
        own_fresh[1],
        preferred_element_type=jnp.float32,
    )
    attended = (numer / mass[..., None]).astype(jnp.bfloat16).reshape(steps_n, rows_dev, width_dev)
    gathered = lax.all_gather(attended, "sub", axis=1, tiled=True)
    samples = gathered.shape[1]
    local_width = out_weight.shape[1]
    head_rows_in = gathered.reshape(steps_n * samples, heads_dev, DH)
    head_weights = out_weight.reshape(heads_dev, DH, local_width)
    scale_a = jnp.repeat(jnp.exp2(-scale_in.astype(jnp.float32)), 128)
    scale_b = jnp.repeat(jnp.exp2(-scale_out.astype(jnp.float32)), 128)
    local_a = lax.dynamic_slice_in_dim(scale_a, sub_rank * local_width, local_width, 0)
    local_b = lax.dynamic_slice_in_dim(scale_b, sub_rank * local_width, local_width, 0)
    per_head_term = jnp.einsum(
        "rhd,hdf->rhf", head_rows_in, head_weights, preferred_element_type=jnp.float32
    )
    clipped = jnp.clip(per_head_term / local_a[None, None, :], -127.0, 127.0).sum(1)
    summed = lax.psum_scatter(clipped, "tp", scatter_dimension=1, tiled=True)
    piece_cols = local_width // tp_count
    piece_start = sub_rank * local_width + tp_rank * piece_cols
    piece_a = lax.dynamic_slice_in_dim(scale_a, piece_start, piece_cols, 0)
    piece_b = lax.dynamic_slice_in_dim(scale_b, piece_start, piece_cols, 0)
    levels = jnp.clip(summed * piece_a / piece_b, -127.0, 127.0).astype(jnp.bfloat16)
    all_levels = lax.all_gather(levels, "tp", axis=1, tiled=True)
    restored = all_levels.astype(jnp.float32) * local_b
    hidden = residual.reshape(steps_n * samples, local_width).astype(jnp.float32) + restored
    return hidden.astype(jnp.bfloat16).reshape(steps_n, samples, local_width)


def solution(mesh):
    return jax.shard_map(
        per_device,
        mesh=mesh,
        in_specs=(
            P(None, ("rep", "sub"), "tp"),
            P(None, ("rep", "tp"), None),
            P(None, ("rep", "sub"), "tp", None),
            P(("rep", "sub")),
            P(None, None, ("rep", "sub"), None),
            P("tp", "sub"),
            P(),
            P(),
            P(None, "rep", "sub"),
        ),
        out_specs=P(None, "rep", "sub"),
        check_vma=False,
    )
```

profile of v0, /device:TPU:0, one launch (start us, length us, event | category | flops | bytes accessed | tf_op | source)
XLA Modules:
  0.0 296.8 jit_solution(12583703444207786706)
XLA Ops:
  6.5 4.3 %copy.48 = bf16[2,4,128,1024]{2,1,0,3:T(4,128)(2,1)} copy(bf16[2,4,128,1024]{3,2,1,0:T(8,128)(2,1)} %param.11) | data formatting | bytes 4194304 | tf_op args[2]
  10.8 7.3 %all-to-all-start.1 = ((bf16[8,128,1024]{1,0,2:T(8,128)(2,1)}), bf16[8,128,1024]{1,0,2:T(8,128)(2,1)S(1)}, u32[]{:S(2)}, u32[]{:S(2)}) async-start(bf16[8,128,1024]{1,0,2:T(8,128)(2,1)} %bitcast.78), calls=%async_computation.1 | async-start | bytes 4194304 | tf_op jit(solution)/shard_map/all_to_all | solution.py:41
  18.1 11.3 %copy.46 = bf16[2,1024,1024]{1,0,2:T(2,128)(2,1)} copy(bf16[2,1024,1024]{2,1,0:T(8,128)(2,1)} %param.10) | data formatting | bytes 8388608 | tf_op args[1]
  29.4 36.9 %all-to-all-done.1 = bf16[8,128,1024]{1,0,2:T(8,128)(2,1)S(1)} async-done(((bf16[8,128,1024]{1,0,2:T(8,128)(2,1)}), bf16[8,128,1024]{1,0,2:T(8,128)(2,1)S(1)}, u32[]{:S(2)}, u32[]{:S(2)}) %all-to-all-start.1) | async-done | bytes 2097184 | tf_op jit(solution)/shard_map/all_to_all | solution.py:41
  66.3 4.5 %all-to-all-start = ((bf16[2,1024,1024]{1,0,2:T(2,128)(2,1)}), bf16[2,1024,1024]{1,0,2:T(2,128)(2,1)}, u32[]{:S(2)}, u32[]{:S(2)}) async-start(bf16[2,1024,1024]{1,0,2:T(2,128)(2,1)} %copy.46), calls=%async_computation | async-start | bytes 8388608 | tf_op jit(solution)/shard_map/all_to_all | solution.py:40
  70.9 0.0 reduce-scatter.2.cloned.1.call-start
  71.0 0.1 broadcast_bitcast_fusion.1
  71.1 0.7 constant_dynamic-slice_fusion.1
  71.8 0.1 iota_compare_fusion
  71.9 0.2 fusion.28
  72.1 0.3 copy.49
  72.4 0.1 fusion.27
  72.5 0.7 copy.57
  73.2 0.7 copy.50
  73.9 0.5 fusion.30
  74.4 89.0 %all-to-all-done = bf16[2,1024,1024]{1,0,2:T(2,128)(2,1)} async-done(((bf16[2,1024,1024]{1,0,2:T(2,128)(2,1)}), bf16[2,1024,1024]{1,0,2:T(2,128)(2,1)}, u32[]{:S(2)}, u32[]{:S(2)}) %all-to-all-start) | async-done | bytes 4194336 | tf_op jit(solution)/shard_map/all_to_all | solution.py:40
  163.4 11.2 %copy.47 = bf16[2,1024,8,128]{3,1,2,0:T(8,128)(2,1)} copy(bf16[2,1024,8,128]{1,0,3,2:T(2,128)(2,1)} %bitcast.1) | data formatting | bytes 8388608 | tf_op jit(solution)/shard_map/all_to_all | solution.py:40
  174.6 2.5 fusion.26
  177.2 0.8 fusion.29
  178.0 0.8 fusion.1
  178.8 0.9 fusion.3
  179.7 0.2 fusion.16
  179.9 0.3 fusion.11
  180.2 0.2 fusion.12
  180.5 1.9 all_gather.6
  182.4 13.7 %fusion.6 = f32[16,8192]{1,0:T(8,128)} fusion(f32[8192]{0:T(1024)S(1)} %dynamic-slice-done, bf16[16,128,8192]{2,1,0:T(8,128)(2,1)} %bitcast.86, bf16[16,16,128]{2,1,0:T(8,128)(2,1)S(1)} %bitcast.85), kind=kOutput, calls=%fused_computation.8 | convolution fusion | flops 543031296 | bytes 34177024 | tf_op jit(solution)/shard_map/rhd,hdf->rhf/dot_general | solution.py:89
  196.2 0.0 reduce-scatter.2.cloned.1.call-update
  196.2 0.1 broadcast_bitcast_fusion
  196.4 61.0 %reduce-scatter.2.cloned.1.call-done = f32[16,1024]{1,0:T(8,128)} async-done(((f32[16,8192]{1,0:T(8,128)}), f32[16,1024]{1,0:T(8,128)}) %reduce-scatter.2.cloned.1.call-update) | async-done | bytes 65552 | tf_op jit(solution)/shard_map/reduce_scatter | solution.py:93
  257.4 0.9 clamp_convert_fusion
  258.2 30.9 %all_gather.7 = bf16[16,8192]{1,0:T(8,128)(2,1)S(1)} all-gather(bf16[16,1024]{1,0:T(8,128)(2,1)S(1)} %clamp_convert_fusion), channel_id=1, replica_groups=mesh['rep'=2,'tp'=8,'sub'=2] {'tp'}, dimensions={1}, use_global_device_ids=true | all-gather | bytes 294912 | tf_op jit(solution)/shard_map/all_gather | solution.py:99
  289.2 0.8 fusion.18
  (31 shorter events, 0.2 us)
Async XLA Ops:
  10.8 55.5 %all-to-all-start.1 = ((bf16[8,128,1024]{1,0,2:T(8,128)(2,1)}), bf16[8,128,1024]{1,0,2:T(8,128)(2,1)S(1)}, u32[]{:S(2)}, u32[]{:S(2)}) async-start(bf16[8,128,1024]{1,0,2:T(8,128)(2,1)} %bitcast.78), calls=%async_computation.1 | async-start | bytes 4194304 | tf_op jit(solution)/shard_map/all_to_all | solution.py:41
  29.4 41.5 %copy-start.3 = (bf16[2,4,2048]{2,1,0:T(4,128)(2,1)S(1)}, bf16[2,4,2048]{2,1,0:T(4,128)(2,1)}, u32[]{:S(2)}) copy-start(bf16[2,4,2048]{2,1,0:T(4,128)(2,1)} %param.9) | copy-start | bytes 98308
  29.4 41.6 %copy-start.5 = (s32[128]{0:T(128)S(1)}, s32[128]{0:T(128)}, u32[]{:S(2)}) copy-start(s32[128]{0:T(128)} %param.15) | copy-start | bytes 1540
  29.4 42.4 %copy-start.4 = (s32[4]{0:T(128)S(1)}, s32[4]{0:T(128)}, u32[]{:S(2)}) copy-start(s32[4]{0:T(128)} %param.12) | copy-start | bytes 52
  66.3 97.1 %all-to-all-start = ((bf16[2,1024,1024]{1,0,2:T(2,128)(2,1)}), bf16[2,1024,1024]{1,0,2:T(2,128)(2,1)}, u32[]{:S(2)}, u32[]{:S(2)}) async-start(bf16[2,1024,1024]{1,0,2:T(2,128)(2,1)} %copy.46), calls=%async_computation | async-start | bytes 8388608 | tf_op jit(solution)/shard_map/all_to_all | solution.py:40
  70.9 186.5 %reduce-scatter.2.cloned.1.call-start = ((), (), s32[]{:S(2)}) async-start(), calls=%async_computation.3 | async-start | bytes 589824 | tf_op jit(solution)/shard_map/reduce_scatter | solution.py:93
  71.1 1.5 copy-start.1
  178.8 3.6 %dynamic-slice-start = ((f32[16384]{0:T(1024)}, s32[]{:T(128)}), f32[8192]{0:T(1024)S(1)}, s32[]{:S(2)}) async-start(f32[16384]{0:T(1024)} %copy-done.1, s32[]{:T(128)} %select_n.29), calls=%async_computation.4 | async-start | bytes 66048 | tf_op jit(solution)/shard_map/dynamic_slice | solution.py:87
  182.4 13.8 %copy-start.6 = (s32[128]{0:T(128)S(1)}, s32[128]{0:T(128)}, u32[]{:S(2)}) copy-start(s32[128]{0:T(128)} %param.16) | copy-start | bytes 1540
  182.4 13.9 %copy-start.2 = (f32[16384]{0:T(1024)S(1)}, f32[16384]{0:T(1024)}, u32[]{:S(2)}) copy-start(f32[16384]{0:T(1024)} %copy-done.1) | copy-start | bytes 196612
  182.4 106.7 %copy-start = (bf16[2,8,8192]{2,1,0:T(8,128)(2,1)S(1)}, bf16[2,8,8192]{2,1,0:T(8,128)(2,1)}, u32[]{:S(2)}) copy-start(bf16[2,8,8192]{2,1,0:T(8,128)(2,1)} %param.17) | copy-start | bytes 786436
Sparse Core Ops, SparseCore 0:
  196.3 61.0 reduce-scatter.1
where the time goes:
time: 298 us; the launch traced here: 297 us
  waiting for transfers between devices  187 us (63%)
  blocking collectives  32.8 us (11%)
  local copies, waits for them, and re-layouts  32.1 us (11%)
  matrix products  16.6 us (6%)
  between operations  13.7 us (5%)
  starting transfers between devices  11.8 us (4%)
    all_to_all x1, waiting for transfers between devices, per_device(): lax.all_to_all(spread_prompt, 'tp', split_axis=2, concat_axis=1, tiled=True)  89 us
    reduce_scatter x1, waiting for transfers between devices, per_device(): summed = lax.psum_scatter(clipped, 'tp', scatter_dimension=1, tiled=True)  61 us
    all_to_all x1, waiting for transfers between devices, per_device(): lax.all_to_all(spread_tail, 'tp', split_axis=2, concat_axis=1, tiled=True)  36.9 us
    all_gather x1, blocking collectives, per_device(): all_levels = lax.all_gather(levels, 'tp', axis=1, tiled=True)  30.9 us
    unnamed x17, local copies, waits for them, and re-layouts  15.7 us
    dot_general x1, matrix products, per_device(): jnp.einsum('rhd,hdf->rhf', head_rows_in, head_weights, preferred_element_...  13.7 us
    all_to_all x1, local copies, waits for them, and re-layouts, per_device(): lax.all_to_all(spread_prompt, 'tp', split_axis=2, concat_axis=1, tiled=True)  11.2 us
    all_to_all x1, starting transfers between devices, per_device(): lax.all_to_all(spread_tail, 'tp', split_axis=2, concat_axis=1, tiled=True)  7.25 us
  transfers between devices with their start and end apart: 3, of which 3 were waited for; matrix products, arithmetic and copies ran while one was open for 5% of the time, Pallas kernels for 0%

commit v1 on v0

--- a/solution.py
+++ b/solution.py
@@ -8,9 +8,37 @@
 NEG_FILL = -1e30
 
 
+def end_patches(here_x, dimension_no):
+    here_x = jnp.moveaxis(here_x, 0, dimension_no)
+    z2 = here_x.shape
+    big = here_x.reshape(
+        *z2[:dimension_no], z2[dimension_no] * z2[dimension_no + 1], *z2[dimension_no + 2 :]
+    )
+    return big
+
+
+def draft_keys(tile_in, a_name):
+    degree = lax.axis_size(a_name)
+    current_block = tile_in[None]
+    for at in range(degree.bit_length() - 1):
+        extra = 1 << at
+        local_next = lax.ppermute(current_block, a_name, [(dd, dd ^ extra) for dd in range(degree)])
+        value_now = jnp.stack([current_block, local_next])
+        d_next = lax.axis_index(a_name) >> at & 1
+        current_block = jnp.where(d_next == 0, value_now, value_now[::-1]).reshape(
+            -1, *tile_in.shape
+        )
+    return current_block
+
+
 def per_device(
     queries, prefix_kv, tail_kv, tail_lengths, fresh_kv, out_weight, scale_in, scale_out, residual
 ):
+
+    def _update_ends(m, mine_x, d0):
+        h_now = end_patches(draft_keys(m, mine_x), d0)
+        return h_now
+
     steps_n, rows_dev, width_dev = queries.shape
     heads_dev = width_dev // DH
     tp_count = lax.axis_size("tp")
@@ -96,7 +124,7 @@
     piece_a = lax.dynamic_slice_in_dim(scale_a, piece_start, piece_cols, 0)
     piece_b = lax.dynamic_slice_in_dim(scale_b, piece_start, piece_cols, 0)
     levels = jnp.clip(summed * piece_a / piece_b, -127.0, 127.0).astype(jnp.bfloat16)
-    all_levels = lax.all_gather(levels, "tp", axis=1, tiled=True)
+    all_levels = _update_ends(levels, "tp", 1)
     restored = all_levels.astype(jnp.float32) * local_b
     hidden = residual.reshape(steps_n * samples, local_width).astype(jnp.float32) + restored
     return hidden.astype(jnp.bfloat16).reshape(steps_n, samples, local_width)

time: 298 us -> 284 us (0.953)
  blocking collectives: 32.8 us -> 1.85 us
  waiting for transfers between devices: 187 us -> 199 us
  starting transfers between devices: 11.8 us -> 15.5 us
    all_gather x1 -> x0, blocking collectives: 30.9 us -> none  [per_device(): all_levels = lax.all_gather(levels, 'tp', axis=1, tiled=True)]
    ppermute x0 -> x3, waiting for transfers between devices: none -> 12.6 us  [draft_keys(): lax.ppermute(current_block, a_name, [(dd, dd ^ extra) for dd in range(deg...]
    ppermute x0 -> x3, starting transfers between devices: none -> 3.61 us  [draft_keys(): lax.ppermute(current_block, a_name, [(dd, dd ^ extra) for dd in range(deg...]
  transfers between devices with their start and end apart: 3 -> 6, of which waited for: 3 -> 6; matrix products, arithmetic and copies ran while one was open for 5% -> 6% of each run, Pallas kernels for 0% -> 0%
where the time goes in v1:
time: 284 us; the launch traced here: 283 us
  waiting for transfers between devices  199 us (70%)
  local copies, waits for them, and re-layouts  32.6 us (11%)
  matrix products  16.6 us (6%)
  starting transfers between devices  15.5 us (5%)
  between operations  13.7 us (5%)
  other arithmetic  3.8 us (1%)
    all_to_all x1, waiting for transfers between devices, per_device(): lax.all_to_all(spread_prompt, 'tp', split_axis=2, concat_axis=1, tiled=True)  89 us
    reduce_scatter x1, waiting for transfers between devices, per_device(): summed = lax.psum_scatter(clipped, 'tp', scatter_dimension=1, tiled=True)  61 us
    all_to_all x1, waiting for transfers between devices, per_device(): lax.all_to_all(spread_tail, 'tp', split_axis=2, concat_axis=1, tiled=True)  36.9 us
    unnamed x17, local copies, waits for them, and re-layouts  15.7 us
    dot_general x1, matrix products, per_device(): jnp.einsum('rhd,hdf->rhf', head_rows_in, head_weights, preferred_element_...  13.7 us
    ppermute x3, waiting for transfers between devices, draft_keys(): lax.ppermute(current_block, a_name, [(dd, dd ^ extra) for dd in range(deg...  12.6 us
    all_to_all x1, local copies, waits for them, and re-layouts, per_device(): lax.all_to_all(spread_prompt, 'tp', split_axis=2, concat_axis=1, tiled=True)  11.2 us
    all_to_all x1, starting transfers between devices, per_device(): lax.all_to_all(spread_tail, 'tp', split_axis=2, concat_axis=1, tiled=True)  7.25 us
  transfers between devices with their start and end apart: 6, of which 6 were waited for; matrix products, arithmetic and copies ran while one was open for 6% of the time, Pallas kernels for 0%

profile of v1, /device:TPU:0, one launch (start us, length us, event | category | flops | bytes accessed | tf_op | source)
XLA Modules:
  0.0 283.5 jit_solution(3837956957820398080)
XLA Ops:
  6.5 4.3 %copy.52 = bf16[2,4,128,1024]{2,1,0,3:T(4,128)(2,1)} copy(bf16[2,4,128,1024]{3,2,1,0:T(8,128)(2,1)} %param.11) | data formatting | bytes 4194304 | tf_op args[2]
  10.8 7.3 %all-to-all-start.1 = ((bf16[8,128,1024]{1,0,2:T(8,128)(2,1)}), bf16[8,128,1024]{1,0,2:T(8,128)(2,1)S(1)}, u32[]{:S(2)}, u32[]{:S(2)}) async-start(bf16[8,128,1024]{1,0,2:T(8,128)(2,1)} %bitcast.92), calls=%async_computation.1 | async-start | bytes 4194304 | tf_op jit(solution)/shard_map/all_to_all | solution.py:69
  18.1 11.3 %copy.50 = bf16[2,1024,1024]{1,0,2:T(2,128)(2,1)} copy(bf16[2,1024,1024]{2,1,0:T(8,128)(2,1)} %param.10) | data formatting | bytes 8388608 | tf_op args[1]
  29.4 36.9 %all-to-all-done.1 = bf16[8,128,1024]{1,0,2:T(8,128)(2,1)S(1)} async-done(((bf16[8,128,1024]{1,0,2:T(8,128)(2,1)}), bf16[8,128,1024]{1,0,2:T(8,128)(2,1)S(1)}, u32[]{:S(2)}, u32[]{:S(2)}) %all-to-all-start.1) | async-done | bytes 2097184 | tf_op jit(solution)/shard_map/all_to_all | solution.py:69
  66.3 4.6 %all-to-all-start = ((bf16[2,1024,1024]{1,0,2:T(2,128)(2,1)}), bf16[2,1024,1024]{1,0,2:T(2,128)(2,1)}, u32[]{:S(2)}, u32[]{:S(2)}) async-start(bf16[2,1024,1024]{1,0,2:T(2,128)(2,1)} %copy.50), calls=%async_computation | async-start | bytes 8388608 | tf_op jit(solution)/shard_map/all_to_all | solution.py:68
  71.1 0.7 constant_dynamic-slice_fusion.1
  71.9 0.2 fusion.28
  72.1 0.3 copy.53
  72.5 0.7 copy.61
  73.2 0.7 copy.54
  73.9 0.5 fusion.30
  74.4 89.0 %all-to-all-done = bf16[2,1024,1024]{1,0,2:T(2,128)(2,1)} async-done(((bf16[2,1024,1024]{1,0,2:T(2,128)(2,1)}), bf16[2,1024,1024]{1,0,2:T(2,128)(2,1)}, u32[]{:S(2)}, u32[]{:S(2)}) %all-to-all-start) | async-done | bytes 4194336 | tf_op jit(solution)/shard_map/all_to_all | solution.py:68
  163.4 11.2 %copy.51 = bf16[2,1024,8,128]{3,1,2,0:T(8,128)(2,1)} copy(bf16[2,1024,8,128]{1,0,3,2:T(2,128)(2,1)} %bitcast) | data formatting | bytes 8388608 | tf_op jit(solution)/shard_map/all_to_all | solution.py:68
  174.6 2.5 fusion.26
  177.2 0.8 fusion.29
  178.0 0.8 fusion.1
  178.7 0.9 fusion.3
  179.7 0.2 fusion.15
  179.9 0.3 fusion.11
  180.5 1.9 all_gather.3
  182.4 13.7 %fusion.6 = f32[16,8192]{1,0:T(8,128)} fusion(f32[8192]{0:T(1024)S(1)} %dynamic-slice-done, bf16[16,128,8192]{2,1,0:T(8,128)(2,1)} %bitcast.106, bf16[16,16,128]{2,1,0:T(8,128)(2,1)S(1)} %bitcast.103), kind=kOutput, calls=%fused_computation.8 | convolution fusion | flops 543031296 | bytes 34177024 | tf_op jit(solution)/shard_map/rhd,hdf->rhf/dot_general | solution.py:117
  196.3 61.0 %reduce-scatter.2.cloned.1.call-done = f32[16,1024]{1,0:T(8,128)} async-done(((f32[16,8192]{1,0:T(8,128)}), f32[16,1024]{1,0:T(8,128)}) %reduce-scatter.2.cloned.1.call-update) | async-done | bytes 65552 | tf_op jit(solution)/shard_map/reduce_scatter | solution.py:121
  257.3 0.9 fusion.38
  258.2 1.4 collective-permute-start
  259.5 0.9 fusion.37
  260.4 1.7 collective-permute-done
  262.2 1.4 collective-permute-start.1
  263.6 4.3 %collective-permute-done.1 = bf16[2,16,1024]{2,1,0:T(8,128)(2,1)S(1)} collective-permute-done((bf16[2,16,1024]{2,1,0:T(8,128)(2,1)S(1)}, bf16[2,16,1024]{2,1,0:T(8,128)(2,1)S(1)}, u32[]{:S(2)}, u32[]{:S(2)}) %collective-permute-start.1) | collective-permute-done | bytes 65568 | tf_op jit(solution)/shard_map/ppermute | solution.py:25
  267.9 0.8 collective-permute-start.2
  268.8 6.5 %collective-permute-done.2 = bf16[4,16,1024]{2,1,0:T(8,128)(2,1)S(1)} collective-permute-done((bf16[4,16,1024]{2,1,0:T(8,128)(2,1)S(1)}, bf16[4,16,1024]{2,1,0:T(8,128)(2,1)S(1)}, u32[]{:S(2)}, u32[]{:S(2)}) %collective-permute-start.2) | collective-permute-done | bytes 131104 | tf_op jit(solution)/shard_map/ppermute | solution.py:25
  275.4 0.3 copy.109
  275.9 0.8 add_convert_fusion
  (46 shorter events, 1.1 us)
Async XLA Ops:
  10.8 55.5 %all-to-all-start.1 = ((bf16[8,128,1024]{1,0,2:T(8,128)(2,1)}), bf16[8,128,1024]{1,0,2:T(8,128)(2,1)S(1)}, u32[]{:S(2)}, u32[]{:S(2)}) async-start(bf16[8,128,1024]{1,0,2:T(8,128)(2,1)} %bitcast.92), calls=%async_computation.1 | async-start | bytes 4194304 | tf_op jit(solution)/shard_map/all_to_all | solution.py:69
  29.4 41.5 %copy-start.3 = (bf16[2,4,2048]{2,1,0:T(4,128)(2,1)S(1)}, bf16[2,4,2048]{2,1,0:T(4,128)(2,1)}, u32[]{:S(2)}) copy-start(bf16[2,4,2048]{2,1,0:T(4,128)(2,1)} %param.9) | copy-start | bytes 98308
  29.4 41.6 %copy-start.5 = (s32[128]{0:T(128)S(1)}, s32[128]{0:T(128)}, u32[]{:S(2)}) copy-start(s32[128]{0:T(128)} %param.15) | copy-start | bytes 1540
  29.4 42.4 %copy-start.4 = (s32[4]{0:T(128)S(1)}, s32[4]{0:T(128)}, u32[]{:S(2)}) copy-start(s32[4]{0:T(128)} %param.12) | copy-start | bytes 52
  66.3 97.1 %all-to-all-start = ((bf16[2,1024,1024]{1,0,2:T(2,128)(2,1)}), bf16[2,1024,1024]{1,0,2:T(2,128)(2,1)}, u32[]{:S(2)}, u32[]{:S(2)}) async-start(bf16[2,1024,1024]{1,0,2:T(2,128)(2,1)} %copy.50), calls=%async_computation | async-start | bytes 8388608 | tf_op jit(solution)/shard_map/all_to_all | solution.py:68
  70.9 186.4 %reduce-scatter.2.cloned.1.call-start = ((), (), s32[]{:S(2)}) async-start(), calls=%async_computation.3 | async-start | bytes 589824 | tf_op jit(solution)/shard_map/reduce_scatter | solution.py:121
  71.1 1.5 copy-start.1
  178.7 3.6 %dynamic-slice-start = ((f32[16384]{0:T(1024)}, s32[]{:T(128)}), f32[8192]{0:T(1024)S(1)}, s32[]{:S(2)}) async-start(f32[16384]{0:T(1024)} %copy-done.1, s32[]{:T(128)} %select_n.56), calls=%async_computation.4 | async-start | bytes 66048 | tf_op jit(solution)/shard_map/dynamic_slice | solution.py:115
  182.4 13.8 %copy-start.2 = (f32[16384]{0:T(1024)S(1)}, f32[16384]{0:T(1024)}, u32[]{:S(2)}) copy-start(f32[16384]{0:T(1024)} %copy-done.1) | copy-start | bytes 196612
  182.4 13.8 %copy-start.6 = (s32[128]{0:T(128)S(1)}, s32[128]{0:T(128)}, u32[]{:S(2)}) copy-start(s32[128]{0:T(128)} %param.16) | copy-start | bytes 1540
  196.1 79.7 %copy-start = (bf16[2,8,8192]{2,1,0:T(8,128)(2,1)S(1)}, bf16[2,8,8192]{2,1,0:T(8,128)(2,1)}, u32[]{:S(2)}) copy-start(bf16[2,8,8192]{2,1,0:T(8,128)(2,1)} %param.17) | copy-start | bytes 786436
  258.2 4.0 %collective-permute-start = (bf16[1,16,1024]{2,1,0:T(8,128)(2,1)S(1)}, bf16[1,16,1024]{2,1,0:T(8,128)(2,1)S(1)}, u32[]{:S(2)}, u32[]{:S(2)}) collective-permute-start(bf16[1,16,1024]{2,1,0:T(8,128)(2,1)S(1)} %fusion.38), channel_id=1, source_target_pairs={{0,2},{2,0},{4,6},{6,4},{8,10},{10,8},{12,14},{14,12},{1,3},{3,1},... | collective-permute-start | bytes 98312 | tf_op jit(solution)/shard_map/ppermute | solution.py:25
  262.2 5.7 %collective-permute-start.1 = (bf16[2,16,1024]{2,1,0:T(8,128)(2,1)S(1)}, bf16[2,16,1024]{2,1,0:T(8,128)(2,1)S(1)}, u32[]{:S(2)}, u32[]{:S(2)}) collective-permute-start(bf16[2,16,1024]{2,1,0:T(8,128)(2,1)S(1)} %get-tuple-element.12), channel_id=1, source_target_pairs={{0,4},{2,6},{4,0},{6,2},{8,12},{10,14},{12,8},{14,10},{1,5},{3,7},... | collective-permute-start | bytes 196616 | tf_op jit(solution)/shard_map/ppermute | solution.py:25
  267.9 7.3 %collective-permute-start.2 = (bf16[4,16,1024]{2,1,0:T(8,128)(2,1)S(1)}, bf16[4,16,1024]{2,1,0:T(8,128)(2,1)S(1)}, u32[]{:S(2)}, u32[]{:S(2)}) collective-permute-start(bf16[4,16,1024]{2,1,0:T(8,128)(2,1)S(1)} %bitcast.99), channel_id=1, source_target_pairs={{0,8},{2,10},{4,12},{6,14},{8,0},{10,2},{12,4},{14,6},{1,9},{3,11}... | collective-permute-start | bytes 393224 | tf_op jit(solution)/shard_map/ppermute | solution.py:25
Sparse Core Ops, SparseCore 0:
  196.3 60.9 reduce-scatter.1
